TPU v7x, 512 devices: a whole 4x4x16 slice. The times are simulated.
512 devices in a mesh: band: 256 (over x_hi, y, z, core), pair: 2 (over x_lo).
Axes of the slice: x: 4 (x_hi: 2, x_lo: 2; x = x_hi * 2 + x_lo), y: 4, z: 16, core: 2. Of those that a mesh axis runs over, the one named last changes fastest.
Arguments:
- frame1: bfloat16 [256, 768, 256], P('band', 'pair'), parts along dimension 1, may hold values from -6 to 6, as said below
- frame2: bfloat16 [256, 768, 256], P('band', 'pair'), parts along dimension 1, may hold values from -6 to 6, as said below
- context: bfloat16 [256, 768, 128], P('band', 'pair'), parts along dimension 1, may hold values from -6 to 6
- hidden_init: bfloat16 [256, 768, 128], P('band', 'pair'), parts along dimension 1, may hold values from -1 to 1
- offsets: int32 [2, 256, 768], P(None, 'band', 'pair'), parts along dimension 2, may hold values from -4 to 4
- w_motion: float32 [3, 128], replicated, may hold values from -3.5 to 3.5
- w_row: bfloat16 [5, 384, 384], replicated, may hold values from -0.125 to 0.125
- w_col: bfloat16 [5, 384, 384], replicated, may hold values from -0.125 to 0.125
Outputs:
- hidden: float32 [256, 768, 128], P('band', 'pair'), parts along dimension 1
- flow: float32 [2, 256, 768], P(None, 'band', 'pair'), parts along dimension 2
There are 2 independent parts, one for each index of `pair`. A program takes and returns all parts, laid end to end along the dimension named above; an argument that names none is the same for every part. Nothing has to cross between parts.
Inputs may be any that keep to these rules, and one draw needn't show every extreme that they name: `frame1`: feature vectors. `frame2`: feature vectors. offsets[0] and offsets[1] are each pixel's teacher lookup offsets, in rows and in strips.
All inputs are finite; a program needn't handle non-finite values.
Results may differ from a plain program's by a relative error of at most 0.0041.
Values may be sent and summed in bfloat16 or wider, within the bound.
No kernel may reach another device: no remote copies, remote signals or barrier semaphores. Data moves between devices by JAX's collectives and lax.ppermute only.
A program may use at most 64 MiB of HBM per device.

v0:
```python
import math
import jax
import jax.numpy as jnp
from jax import lax
from jax.sharding import PartitionSpec as P

ITERS = 2


def passed_along(array, axis, by):
    count = lax.axis_size(axis)
    pairs = [(i, i + by) for i in range(count) if 0 <= i + by < count]
    return lax.ppermute(array, axis, pairs)


def pool_strips(frame2):
    band_rows, image_width, channels = frame2.shape
    blocks = frame2.astype(jnp.float32).reshape(band_rows, image_width // 8, 8, channels)
    return (jnp.sum(blocks, axis=2) / 2.0).astype(jnp.bfloat16)


def lookup_targets(offsets, row_first, total_rows, image_width):
    band_rows = offsets.shape[1]
    pixel_row = (
        row_first
        + jnp.arange(band_rows, dtype=jnp.int32)[:, None]
        + jnp.zeros((1, image_width), jnp.int32)
    )
    pixel_col = jnp.arange(image_width, dtype=jnp.int32)[None, :]
    target_row = pixel_row + offsets[0]
    target_col = pixel_col // 8 + offsets[1]
    inside = (
        (target_row >= 0)
        & (target_row < total_rows)
        & (target_col >= 0)
        & (target_col < image_width // 8)
    )
    target_row = jnp.where(inside, target_row, -1)
    target_col = jnp.where(inside, target_col, -1)
    return (target_row, target_col, pixel_row, pixel_col)


def strip_step(
    state, feature_rows, strip_block, row_zero, total_rows, image_width, target_row, target_col
):
    block_rows, grid_cols, channels = strip_block.shape
    scores = jnp.dot(
        feature_rows,
        strip_block.reshape(block_rows * grid_cols, channels).T,
        preferred_element_type=jnp.float32,
    ) / math.sqrt(channels)
    running_max, denominator, acc_row, acc_col, lookup = state
    new_max = jnp.maximum(running_max, jnp.max(scores, axis=1))
    shrink = jnp.exp(running_max - new_max)
    exponent = jnp.exp(scores - new_max[:, None]).reshape(-1, block_rows, grid_cols)
    strip_row = row_zero + jnp.arange(block_rows, dtype=jnp.int32)
    column_ids = jnp.arange(grid_cols, dtype=jnp.int32)
    row_centre = strip_row.astype(jnp.float32) / total_rows
    col_centre = ((8 * column_ids).astype(jnp.float32) + 3.5) / image_width
    row_weight = jnp.sum(exponent, axis=2)
    col_weight = jnp.sum(exponent, axis=1)
    scores_grid = scores.reshape(-1, block_rows, grid_cols)
    hit = (strip_row[None, :, None] == target_row[:, None, None]) & (
        column_ids[None, None, :] == target_col[:, None, None]
    )
    found = jnp.sum(jnp.where(hit, scores_grid, 0.0), axis=(1, 2))
    return (
        new_max,
        denominator * shrink + jnp.sum(row_weight, axis=1),
        acc_row * shrink + jnp.sum(row_weight * row_centre[None, :], axis=1),
        acc_col * shrink + jnp.sum(col_weight * col_centre[None, :], axis=1),
        lookup + found,
    )


def conv_valid(source, weight, conv_axis):
    out_count = source.shape[conv_axis] - 4
    summed = None
    for kernel_tap in range(5):
        tap_slice = lax.slice_in_dim(source, kernel_tap, kernel_tap + out_count, axis=conv_axis)
        tap_term = jnp.dot(
            tap_slice.reshape(-1, tap_slice.shape[-1]),
            weight[kernel_tap],
            preferred_element_type=jnp.float32,
        )
        summed = tap_term if summed is None else summed + tap_term
    out_shape = tuple(tap_slice.shape[:-1]) + (weight.shape[-1],)
    return summed.reshape(out_shape)


def pad_columns(source):
    return jnp.pad(source, ((0, 0), (2, 2), (0, 0)))


def rows_around(source, depth, mover):
    above = [
        mover(source, offset)
        for offset in list(range(depth, 0, -1)) + list(range(-1, -depth - 1, -1))
    ]
    return jnp.concatenate(above[:depth] + [source] + above[depth:], axis=0)


def row_pass(hidden, from_inputs, weight):
    width_h = hidden.shape[-1]
    hidden_half = lax.optimization_barrier(hidden.astype(jnp.bfloat16))
    gate_pair = jax.nn.sigmoid(
        conv_valid(pad_columns(hidden_half), weight[:, :width_h, : 2 * width_h], 1)
        + from_inputs[..., : 2 * width_h]
    )
    update_gate = gate_pair[..., :width_h]
    reset_gate = gate_pair[..., width_h:]
    gated = (reset_gate * hidden_half.astype(jnp.float32)).astype(jnp.bfloat16)
    candidate = jnp.tanh(
        conv_valid(pad_columns(gated), weight[:, :width_h, 2 * width_h :], 1)
        + from_inputs[..., 2 * width_h :]
    )
    return (1.0 - update_gate) * hidden + update_gate * candidate


def column_pass_each(hidden, from_inputs, weight):
    width_h = hidden.shape[-1]
    hidden_half = lax.optimization_barrier(hidden.astype(jnp.bfloat16))
    hidden_ext = rows_around(
        hidden_half, 2, lambda source, offset: passed_along(source, "band", offset)
    )
    gate_pair = jax.nn.sigmoid(
        conv_valid(hidden_ext, weight[:, :width_h, : 2 * width_h], 0)
        + from_inputs[..., : 2 * width_h]
    )
    update_gate = gate_pair[..., :width_h]
    reset_gate = gate_pair[..., width_h:]
    gated = (reset_gate * hidden_half.astype(jnp.float32)).astype(jnp.bfloat16)
    gated_ext = rows_around(gated, 2, lambda source, offset: passed_along(source, "band", offset))
    candidate = jnp.tanh(
        conv_valid(gated_ext, weight[:, :width_h, 2 * width_h :], 0)
        + from_inputs[..., 2 * width_h :]
    )
    return (1.0 - update_gate) * hidden + update_gate * candidate


def per_device(frame1, frame2, context, hidden_init, offsets, w_motion, w_row, w_col):
    band_rows, image_width, channels = frame1.shape
    total_rows = band_rows * lax.axis_size("band")
    row_first = lax.axis_index("band") * band_rows
    strips = pool_strips(frame2)
    target_row, target_col, pixel_row, pixel_col = lookup_targets(
        offsets, row_first, total_rows, image_width
    )
    pixel_count = band_rows * image_width
    features = frame1.reshape(pixel_count, channels)
    rows_target = target_row.reshape(pixel_count)
    cols_target = target_col.reshape(pixel_count)
    zeros_state = jnp.zeros((pixel_count,), jnp.float32)
    initial = (
        jnp.full((pixel_count,), -jnp.inf, jnp.float32),
        zeros_state,
        zeros_state,
        zeros_state,
        zeros_state,
    )
    state = initial
    arriving = lax.all_gather(strips, "band", axis=0, tiled=True)
    arriving_rows = arriving.shape[0]
    step_rows = min(arriving_rows, 16)
    full_steps = arriving_rows // step_rows
    blocks = arriving.reshape((full_steps, step_rows) + arriving.shape[1:])
    starts = step_rows * jnp.arange(full_steps, dtype=jnp.int32)

    def advance(carry, pieces):
        return (
            strip_step(
                carry,
                features,
                pieces[0],
                pieces[1],
                total_rows,
                image_width,
                rows_target,
                cols_target,
            ),
            None,
        )

    state, unused = lax.scan(advance, state, (blocks, starts))
    running_max, denominator, acc_row, acc_col, lookup = state
    flow_row = (acc_row / denominator).reshape(band_rows, image_width) - pixel_row.astype(
        jnp.float32
    ) / total_rows
    flow_col = (acc_col / denominator).reshape(band_rows, image_width) - pixel_col.astype(
        jnp.float32
    ) / image_width
    lookup = lookup.reshape(band_rows, image_width)
    motion = jax.nn.relu(
        flow_row[..., None] * w_motion[0]
        + flow_col[..., None] * w_motion[1]
        + lookup[..., None] * w_motion[2]
    ).astype(jnp.bfloat16)
    inputs = jnp.concatenate([context, motion], axis=-1)
    width_h = hidden_init.shape[-1]
    from_row = conv_valid(pad_columns(inputs), w_row[:, width_h:, :], 1)
    hidden = hidden_init.astype(jnp.float32)
    inputs_ext = rows_around(inputs, 2, lambda source, offset: passed_along(source, "band", offset))
    from_col = conv_valid(inputs_ext, w_col[:, width_h:, :], 0)
    for iteration in range(ITERS):
        hidden = row_pass(hidden, from_row, w_row)
        hidden = column_pass_each(hidden, from_col, w_col)
    return (hidden, jnp.stack([flow_row, flow_col]))


def solution(mesh):
    return jax.shard_map(
        per_device,
        mesh=mesh,
        in_specs=(
            P("band", "pair", None),
            P("band", "pair", None),
            P("band", "pair", None),
            P("band", "pair", None),
            P(None, "band", "pair"),
            P(),
            P(),
            P(),
        ),
        out_specs=(P("band", "pair", None), P(None, "band", "pair")),
        check_vma=False,
    )
```

profile of v0, /device:TPU:7, one launch (start us, length us, event | category | flops | bytes accessed | tf_op | source)
XLA Modules:
  0.0 416.5 jit_solution(839724236668119955)
XLA Ops:
  7.2 1.2 convert_reduce_fusion
  9.1 0.8 slice_bitcast_fusion.2
  11.3 1.1 fusion.158
  12.4 1.1 convolution_add_fusion.17
  14.0 222.3 %all-gather.3.cloned.1.call-done = bf16[12288,256]{1,0:T(8,128)(2,1)} async-done(((bf16[48,256]{1,0:T(8,128)(2,1)}), bf16[12288,256]{1,0:T(8,128)(2,1)}) %all-gather.3.cloned.1.call-update) | async-done | bytes 6291472 | tf_op jit(solution)/shard_map/all_gather | solution.py:162
  236.2 70.1 %while.19 = (s32[]{:T(128)}, f32[384]{0:T(512)S(1)}, f32[384]{0:T(512)S(1)}, f32[384]{0:T(512)S(1)}, f32[384]{0:T(512)S(1)}, /*index=5*/f32[384]{0:T(512)S(1)}, ...) while((s32[]{:T(128)}, f32[384]{0:T(512)S(1)}, ...), condition=%wide.region_9.10_spmd.clone, body=%wide.region_1.9_spmd.clone.sunk | while | flops 153702400 | bytes 6978856 | solution.py:184
  236.2 1.1 constant_dynamic-slice_fusion.2
  240.6 1.0 constant_dynamic-slice_fusion.2
  245.0 1.0 constant_dynamic-slice_fusion.2
  249.4 1.0 constant_dynamic-slice_fusion.2
  253.8 1.0 constant_dynamic-slice_fusion.2
  258.2 1.0 constant_dynamic-slice_fusion.2
  262.5 1.0 constant_dynamic-slice_fusion.2
  266.9 1.0 constant_dynamic-slice_fusion.2
  271.3 1.0 constant_dynamic-slice_fusion.2
  275.7 1.0 constant_dynamic-slice_fusion.2
  280.1 1.0 constant_dynamic-slice_fusion.2
  284.4 1.0 constant_dynamic-slice_fusion.2
  288.8 1.0 constant_dynamic-slice_fusion.2
  293.2 1.0 constant_dynamic-slice_fusion.2
  297.6 1.0 constant_dynamic-slice_fusion.2
  302.0 1.0 constant_dynamic-slice_fusion.2
  309.2 3.3 collective-permute-start.1
  312.5 2.2 collective-permute-start
  314.7 8.8 %collective-permute-start.3 = (bf16[1,384,128]{2,1,0:T(8,128)(2,1)S(1)}, bf16[1,384,128]{2,1,0:T(8,128)(2,1)S(1)}, u32[]{:S(2)}, u32[]{:S(2)}) collective-permute-start(bf16[1,384,128]{2,1,0:T(8,128)(2,1)S(1)} %get-tuple-element.142), channel_id=1, source_target_pairs={{4,0},{6,2},{8,4},{10,6},{12,8},{14,10},{16,12},{18,14},{20,16},{2... | collective-permute-start | bytes 294920 | tf_op jit(solution)/shard_map/ppermute | solution.py:13
  323.5 1.9 collective-permute-start.2
  325.4 3.6 collective-permute-start.5
  330.1 1.9 collective-permute-start.4
  332.3 9.1 %collective-permute-start.7 = (bf16[1,384,256]{2,1,0:T(8,128)(2,1)S(1)}, bf16[1,384,256]{2,1,0:T(8,128)(2,1)S(1)}, u32[]{:S(2)}, u32[]{:S(2)}) collective-permute-start(bf16[1,384,256]{2,1,0:T(8,128)(2,1)S(1)} %pad_maximum_fusion), channel_id=1, source_target_pairs={{4,0},{6,2},{8,4},{10,6},{12,8},{14,10},{16,12},{18,14},{20,16},{2... | collective-permute-start | bytes 589832 | tf_op jit(solution)/shard_map/ppermute | solution.py:13
  341.6 1.9 collective-permute-start.6
  344.2 1.8 collective-permute-done.7
  346.3 2.2 collective-permute-done.6
  349.1 1.9 collective-permute-start.9
  351.2 1.9 collective-permute-start.8
  353.1 9.1 %collective-permute-start.11 = (bf16[1,384,128]{2,1,0:T(8,128)(2,1)S(1)}, bf16[1,384,128]{2,1,0:T(8,128)(2,1)S(1)}, u32[]{:S(2)}, u32[]{:S(2)}) collective-permute-start(bf16[1,384,128]{2,1,0:T(8,128)(2,1)S(1)} %fusion.60), channel_id=1, source_target_pairs={{4,0},{6,2},{8,4},{10,6},{12,8},{14,10},{16,12},{18,14},{20,16},{2... | collective-permute-start | bytes 294920 | tf_op jit(solution)/shard_map/ppermute | solution.py:13
  362.2 3.0 collective-permute-start.10
  365.7 2.5 collective-permute-done.10
  370.3 1.9 collective-permute-start.13
  372.5 1.9 collective-permute-start.12
  374.4 9.1 %collective-permute-start.15 = (bf16[1,384,128]{2,1,0:T(8,128)(2,1)S(1)}, bf16[1,384,128]{2,1,0:T(8,128)(2,1)S(1)}, u32[]{:S(2)}, u32[]{:S(2)}) collective-permute-start(bf16[1,384,128]{2,1,0:T(8,128)(2,1)S(1)} %get-tuple-element.146), channel_id=1, source_target_pairs={{4,0},{6,2},{8,4},{10,6},{12,8},{14,10},{16,12},{18,14},{20,16},{2... | collective-permute-start | bytes 294920 | tf_op jit(solution)/shard_map/ppermute | solution.py:13
  383.5 3.0 collective-permute-start.14
  387.1 2.3 collective-permute-done.14
  389.7 1.9 collective-permute-start.17
  391.8 1.9 collective-permute-start.16
  393.7 9.1 %collective-permute-start.19 = (bf16[1,384,128]{2,1,0:T(8,128)(2,1)S(1)}, bf16[1,384,128]{2,1,0:T(8,128)(2,1)S(1)}, u32[]{:S(2)}, u32[]{:S(2)}) collective-permute-start(bf16[1,384,128]{2,1,0:T(8,128)(2,1)S(1)} %fusion.58), channel_id=1, source_target_pairs={{4,0},{6,2},{8,4},{10,6},{12,8},{14,10},{16,12},{18,14},{20,16},{2... | collective-permute-start | bytes 294920 | tf_op jit(solution)/shard_map/ppermute | solution.py:13
  402.8 3.0 collective-permute-start.18
  406.3 2.4 collective-permute-done.18
  408.8 0.9 multiply_add_fusion
  (365 shorter events, 65.1 us)
Async XLA Ops:
  7.2 6.4 %copy-start.1 = (bf16[1,384,128]{2,1,0:T(8,128)(2,1)S(1)}, bf16[1,384,128]{2,1,0:T(8,128)(2,1)}, u32[]{:S(2)}) copy-start(bf16[1,384,128]{2,1,0:T(8,128)(2,1)} %param.13) | copy-start | bytes 294916
  7.2 6.4 %copy-start.3 = (bf16[5,384,384]{2,1,0:T(8,128)(2,1)S(1)}, bf16[5,384,384]{2,1,0:T(8,128)(2,1)}, u32[]{:S(2)}) copy-start(bf16[5,384,384]{2,1,0:T(8,128)(2,1)} %param.16) | copy-start | bytes 4423684
  7.2 229.0 %all-gather.3.cloned.1.call-start = ((), (), s32[]{:S(2)}) async-start(), calls=%async_computation | async-start | bytes 6316032 | tf_op jit(solution)/shard_map/all_gather | solution.py:162
  12.4 223.8 %copy-start = (bf16[1,384,256]{2,1,0:T(8,128)(2,1)S(1)}, bf16[1,384,256]{2,1,0:T(8,128)(2,1)}, u32[]{:S(2)}) copy-start(bf16[1,384,256]{2,1,0:T(8,128)(2,1)} %param.10) | copy-start | bytes 589828
  236.2 70.3 %copy-start.4 = (bf16[1,384,128]{2,1,0:T(8,128)(2,1)S(1)}, bf16[1,384,128]{2,1,0:T(8,128)(2,1)}, u32[]{:S(2)}) copy-start(bf16[1,384,128]{2,1,0:T(8,128)(2,1)} %param.12) | copy-start | bytes 294916
  308.3 20.8 %copy-start.2 = (bf16[5,384,384]{2,1,0:T(8,128)(2,1)S(1)}, bf16[5,384,384]{2,1,0:T(8,128)(2,1)}, u32[]{:S(2)}) copy-start(bf16[5,384,384]{2,1,0:T(8,128)(2,1)} %param.17) | copy-start | bytes 4423684
  309.2 21.0 %collective-permute-start.1 = (bf16[1,384,128]{2,1,0:T(8,128)(2,1)S(1)}, bf16[1,384,128]{2,1,0:T(8,128)(2,1)S(1)}, u32[]{:S(2)}, u32[]{:S(2)}) collective-permute-start(bf16[1,384,128]{2,1,0:T(8,128)(2,1)S(1)} %get-tuple-element.142), channel_id=1, source_target_pairs={{0,2},{2,4},{4,6},{6,8},{8,10},{10,12},{12,14},{14,16},{16,18},{18... | collective-permute-start | bytes 294920 | tf_op jit(solution)/shard_map/ppermute | solution.py:13
  312.5 19.8 %collective-permute-start = (bf16[1,384,128]{2,1,0:T(8,128)(2,1)S(1)}, bf16[1,384,128]{2,1,0:T(8,128)(2,1)S(1)}, u32[]{:S(2)}, u32[]{:S(2)}) collective-permute-start(bf16[1,384,128]{2,1,0:T(8,128)(2,1)S(1)} %get-tuple-element.142), channel_id=1, source_target_pairs={{0,4},{2,6},{4,8},{6,10},{8,12},{10,14},{12,16},{14,18},{16,20},{1... | collective-permute-start | bytes 294920 | tf_op jit(solution)/shard_map/ppermute | solution.py:13
  314.7 26.8 %collective-permute-start.3 = (bf16[1,384,128]{2,1,0:T(8,128)(2,1)S(1)}, bf16[1,384,128]{2,1,0:T(8,128)(2,1)S(1)}, u32[]{:S(2)}, u32[]{:S(2)}) collective-permute-start(bf16[1,384,128]{2,1,0:T(8,128)(2,1)S(1)} %get-tuple-element.142), channel_id=1, source_target_pairs={{4,0},{6,2},{8,4},{10,6},{12,8},{14,10},{16,12},{18,14},{20,16},{2... | collective-permute-start | bytes 294920 | tf_op jit(solution)/shard_map/ppermute | solution.py:13
  323.5 25.3 %collective-permute-start.2 = (bf16[1,384,128]{2,1,0:T(8,128)(2,1)S(1)}, bf16[1,384,128]{2,1,0:T(8,128)(2,1)S(1)}, u32[]{:S(2)}, u32[]{:S(2)}) collective-permute-start(bf16[1,384,128]{2,1,0:T(8,128)(2,1)S(1)} %get-tuple-element.142), channel_id=1, source_target_pairs={{2,0},{4,2},{6,4},{8,6},{10,8},{12,10},{14,12},{16,14},{18,16},{20... | collective-permute-start | bytes 294920 | tf_op jit(solution)/shard_map/ppermute | solution.py:13
  325.4 18.3 %collective-permute-start.5 = (bf16[1,384,256]{2,1,0:T(8,128)(2,1)S(1)}, bf16[1,384,256]{2,1,0:T(8,128)(2,1)S(1)}, u32[]{:S(2)}, u32[]{:S(2)}) collective-permute-start(bf16[1,384,256]{2,1,0:T(8,128)(2,1)S(1)} %pad_maximum_fusion), channel_id=1, source_target_pairs={{0,2},{2,4},{4,6},{6,8},{8,10},{10,12},{12,14},{14,16},{16,18},{18... | collective-permute-start | bytes 589832 | tf_op jit(solution)/shard_map/ppermute | solution.py:13
  330.1 13.8 %collective-permute-start.4 = (bf16[1,384,256]{2,1,0:T(8,128)(2,1)S(1)}, bf16[1,384,256]{2,1,0:T(8,128)(2,1)S(1)}, u32[]{:S(2)}, u32[]{:S(2)}) collective-permute-start(bf16[1,384,256]{2,1,0:T(8,128)(2,1)S(1)} %pad_maximum_fusion), channel_id=1, source_target_pairs={{0,4},{2,6},{4,8},{6,10},{8,12},{10,14},{12,16},{14,18},{16,20},{1... | collective-permute-start | bytes 589832 | tf_op jit(solution)/shard_map/ppermute | solution.py:13
  332.3 13.8 %collective-permute-start.7 = (bf16[1,384,256]{2,1,0:T(8,128)(2,1)S(1)}, bf16[1,384,256]{2,1,0:T(8,128)(2,1)S(1)}, u32[]{:S(2)}, u32[]{:S(2)}) collective-permute-start(bf16[1,384,256]{2,1,0:T(8,128)(2,1)S(1)} %pad_maximum_fusion), channel_id=1, source_target_pairs={{4,0},{6,2},{8,4},{10,6},{12,8},{14,10},{16,12},{18,14},{20,16},{2... | collective-permute-start | bytes 589832 | tf_op jit(solution)/shard_map/ppermute | solution.py:13
  341.6 7.0 %collective-permute-start.6 = (bf16[1,384,256]{2,1,0:T(8,128)(2,1)S(1)}, bf16[1,384,256]{2,1,0:T(8,128)(2,1)S(1)}, u32[]{:S(2)}, u32[]{:S(2)}) collective-permute-start(bf16[1,384,256]{2,1,0:T(8,128)(2,1)S(1)} %pad_maximum_fusion), channel_id=1, source_target_pairs={{2,0},{4,2},{6,4},{8,6},{10,8},{12,10},{14,12},{16,14},{18,16},{20... | collective-permute-start | bytes 589832 | tf_op jit(solution)/shard_map/ppermute | solution.py:13
  349.1 16.1 %collective-permute-start.9 = (bf16[1,384,128]{2,1,0:T(8,128)(2,1)S(1)}, bf16[1,384,128]{2,1,0:T(8,128)(2,1)S(1)}, u32[]{:S(2)}, u32[]{:S(2)}) collective-permute-start(bf16[1,384,128]{2,1,0:T(8,128)(2,1)S(1)} %fusion.60), channel_id=1, source_target_pairs={{0,2},{2,4},{4,6},{6,8},{8,10},{10,12},{12,14},{14,16},{16,18},{18... | collective-permute-start | bytes 294920 | tf_op jit(solution)/shard_map/ppermute | solution.py:13
  351.2 14.2 %collective-permute-start.8 = (bf16[1,384,128]{2,1,0:T(8,128)(2,1)S(1)}, bf16[1,384,128]{2,1,0:T(8,128)(2,1)S(1)}, u32[]{:S(2)}, u32[]{:S(2)}) collective-permute-start(bf16[1,384,128]{2,1,0:T(8,128)(2,1)S(1)} %fusion.60), channel_id=1, source_target_pairs={{0,4},{2,6},{4,8},{6,10},{8,12},{10,14},{12,16},{14,18},{16,20},{1... | collective-permute-start | bytes 294920 | tf_op jit(solution)/shard_map/ppermute | solution.py:13
  353.1 12.4 %collective-permute-start.11 = (bf16[1,384,128]{2,1,0:T(8,128)(2,1)S(1)}, bf16[1,384,128]{2,1,0:T(8,128)(2,1)S(1)}, u32[]{:S(2)}, u32[]{:S(2)}) collective-permute-start(bf16[1,384,128]{2,1,0:T(8,128)(2,1)S(1)} %fusion.60), channel_id=1, source_target_pairs={{4,0},{6,2},{8,4},{10,6},{12,8},{14,10},{16,12},{18,14},{20,16},{2... | collective-permute-start | bytes 294920 | tf_op jit(solution)/shard_map/ppermute | solution.py:13
  362.2 5.9 %collective-permute-start.10 = (bf16[1,384,128]{2,1,0:T(8,128)(2,1)S(1)}, bf16[1,384,128]{2,1,0:T(8,128)(2,1)S(1)}, u32[]{:S(2)}, u32[]{:S(2)}) collective-permute-start(bf16[1,384,128]{2,1,0:T(8,128)(2,1)S(1)} %fusion.60), channel_id=1, source_target_pairs={{2,0},{4,2},{6,4},{8,6},{10,8},{12,10},{14,12},{16,14},{18,16},{20... | collective-permute-start | bytes 294920 | tf_op jit(solution)/shard_map/ppermute | solution.py:13
  370.3 16.1 %collective-permute-start.13 = (bf16[1,384,128]{2,1,0:T(8,128)(2,1)S(1)}, bf16[1,384,128]{2,1,0:T(8,128)(2,1)S(1)}, u32[]{:S(2)}, u32[]{:S(2)}) collective-permute-start(bf16[1,384,128]{2,1,0:T(8,128)(2,1)S(1)} %get-tuple-element.146), channel_id=1, source_target_pairs={{0,2},{2,4},{4,6},{6,8},{8,10},{10,12},{12,14},{14,16},{16,18},{18... | collective-permute-start | bytes 294920 | tf_op jit(solution)/shard_map/ppermute | solution.py:13
  372.5 14.2 %collective-permute-start.12 = (bf16[1,384,128]{2,1,0:T(8,128)(2,1)S(1)}, bf16[1,384,128]{2,1,0:T(8,128)(2,1)S(1)}, u32[]{:S(2)}, u32[]{:S(2)}) collective-permute-start(bf16[1,384,128]{2,1,0:T(8,128)(2,1)S(1)} %get-tuple-element.146), channel_id=1, source_target_pairs={{0,4},{2,6},{4,8},{6,10},{8,12},{10,14},{12,16},{14,18},{16,20},{1... | collective-permute-start | bytes 294920 | tf_op jit(solution)/shard_map/ppermute | solution.py:13
  374.4 12.5 %collective-permute-start.15 = (bf16[1,384,128]{2,1,0:T(8,128)(2,1)S(1)}, bf16[1,384,128]{2,1,0:T(8,128)(2,1)S(1)}, u32[]{:S(2)}, u32[]{:S(2)}) collective-permute-start(bf16[1,384,128]{2,1,0:T(8,128)(2,1)S(1)} %get-tuple-element.146), channel_id=1, source_target_pairs={{4,0},{6,2},{8,4},{10,6},{12,8},{14,10},{16,12},{18,14},{20,16},{2... | collective-permute-start | bytes 294920 | tf_op jit(solution)/shard_map/ppermute | solution.py:13
  383.5 5.9 %collective-permute-start.14 = (bf16[1,384,128]{2,1,0:T(8,128)(2,1)S(1)}, bf16[1,384,128]{2,1,0:T(8,128)(2,1)S(1)}, u32[]{:S(2)}, u32[]{:S(2)}) collective-permute-start(bf16[1,384,128]{2,1,0:T(8,128)(2,1)S(1)} %get-tuple-element.146), channel_id=1, source_target_pairs={{2,0},{4,2},{6,4},{8,6},{10,8},{12,10},{14,12},{16,14},{18,16},{20... | collective-permute-start | bytes 294920 | tf_op jit(solution)/shard_map/ppermute | solution.py:13
  389.7 16.1 %collective-permute-start.17 = (bf16[1,384,128]{2,1,0:T(8,128)(2,1)S(1)}, bf16[1,384,128]{2,1,0:T(8,128)(2,1)S(1)}, u32[]{:S(2)}, u32[]{:S(2)}) collective-permute-start(bf16[1,384,128]{2,1,0:T(8,128)(2,1)S(1)} %fusion.58), channel_id=1, source_target_pairs={{0,2},{2,4},{4,6},{6,8},{8,10},{10,12},{12,14},{14,16},{16,18},{18... | collective-permute-start | bytes 294920 | tf_op jit(solution)/shard_map/ppermute | solution.py:13
  391.8 14.2 %collective-permute-start.16 = (bf16[1,384,128]{2,1,0:T(8,128)(2,1)S(1)}, bf16[1,384,128]{2,1,0:T(8,128)(2,1)S(1)}, u32[]{:S(2)}, u32[]{:S(2)}) collective-permute-start(bf16[1,384,128]{2,1,0:T(8,128)(2,1)S(1)} %fusion.58), channel_id=1, source_target_pairs={{0,4},{2,6},{4,8},{6,10},{8,12},{10,14},{12,16},{14,18},{16,20},{1... | collective-permute-start | bytes 294920 | tf_op jit(solution)/shard_map/ppermute | solution.py:13
  393.7 12.4 %collective-permute-start.19 = (bf16[1,384,128]{2,1,0:T(8,128)(2,1)S(1)}, bf16[1,384,128]{2,1,0:T(8,128)(2,1)S(1)}, u32[]{:S(2)}, u32[]{:S(2)}) collective-permute-start(bf16[1,384,128]{2,1,0:T(8,128)(2,1)S(1)} %fusion.58), channel_id=1, source_target_pairs={{4,0},{6,2},{8,4},{10,6},{12,8},{14,10},{16,12},{18,14},{20,16},{2... | collective-permute-start | bytes 294920 | tf_op jit(solution)/shard_map/ppermute | solution.py:13
  402.8 5.9 %collective-permute-start.18 = (bf16[1,384,128]{2,1,0:T(8,128)(2,1)S(1)}, bf16[1,384,128]{2,1,0:T(8,128)(2,1)S(1)}, u32[]{:S(2)}, u32[]{:S(2)}) collective-permute-start(bf16[1,384,128]{2,1,0:T(8,128)(2,1)S(1)} %fusion.58), channel_id=1, source_target_pairs={{2,0},{4,2},{6,4},{8,6},{10,8},{12,10},{14,12},{16,14},{18,16},{20... | collective-permute-start | bytes 294920 | tf_op jit(solution)/shard_map/ppermute | solution.py:13
Sparse Core Ops, SparseCore 0:
  13.2 223.0 all-gather.2
where the time goes:
time: 418 us; the launch traced here: 416 us
  waiting for transfers between devices  234 us (56%)
  starting transfers between devices  80.5 us (19%)
  other arithmetic  40.6 us (10%)
  local copies, waits for them, and re-layouts  26.7 us (6%)
  matrix products  19.1 us (5%)
  between operations  14.7 us (4%)
    all_gather x1, waiting for transfers between devices, per_device(): arriving = lax.all_gather(strips, 'band', axis=0, tiled=True)  222 us
    ppermute x20, starting transfers between devices, passed_along(): return lax.ppermute(array, axis, pairs)  80.5 us
    dynamic_slice x32, local copies, waits for them, and re-layouts, per_device(): state, unused = lax.scan(advance, state, (blocks, starts))  25.9 us
    dot_general x50, matrix products, conv_valid(): jnp.dot(tap_slice.reshape(-1, tap_slice.shape[-1]), weight[kernel_tap], p...  12.6 us
    ppermute x20, waiting for transfers between devices, passed_along(): return lax.ppermute(array, axis, pairs)  11.3 us
    div x16, other arithmetic, strip_step(): row_centre = strip_row.astype(jnp.float32) / total_rows  10.4 us
    add x16, other arithmetic, strip_step(): strip_row = row_zero + jnp.arange(block_rows, dtype=jnp.int32)  10.3 us
  transfers between devices with their start and end apart: 21, of which 6 were waited for; matrix products, arithmetic and copies ran while one was open for 2% of the time, Pallas kernels for 0%

commit v1 on v0

--- a/solution.py
+++ b/solution.py
@@ -159,7 +159,9 @@
         zeros_state,
     )
     state = initial
-    arriving = lax.all_gather(strips, "band", axis=0, tiled=True)
+    arriving = jnp.concatenate(
+        lax.all_to_all(jnp.stack([strips] * lax.axis_size("band")), "band", 0, 0), axis=0
+    )
     arriving_rows = arriving.shape[0]
     step_rows = min(arriving_rows, 16)
     full_steps = arriving_rows // step_rows

time: 418 us -> 481 us (1.15)
  waiting for transfers between devices: 234 us -> 280 us
  starting transfers between devices: 80.5 us -> 113 us
  between operations: 14.7 us -> 1.37 us
    all_to_all x0 -> x1, waiting for transfers between devices: none -> 268 us  [per_device(): lax.all_to_all(jnp.stack([strips] * lax.axis_size('band')), 'band', 0, 0)]
    all_gather x1 -> x0, waiting for transfers between devices: 222 us -> none  [per_device(): arriving = lax.all_gather(strips, 'band', axis=0, tiled=True)]
    all_to_all x0 -> x1, starting transfers between devices: none -> 25.6 us  [per_device(): lax.all_to_all(jnp.stack([strips] * lax.axis_size('band')), 'band', 0, 0)]
    ppermute x20, starting transfers between devices: 80.5 us -> 87 us  [passed_along(): return lax.ppermute(array, axis, pairs)]
  transfers between devices with their start and end apart: 21 -> 21, of which waited for: 6 -> 6; matrix products, arithmetic and copies ran while one was open for 2% -> 1% of each run, Pallas kernels for 0% -> 0%
where the time goes in v1:
time: 481 us; the launch traced here: 480 us
  waiting for transfers between devices  280 us (58%)
  starting transfers between devices  113 us (23%)
  other arithmetic  38.4 us (8%)
  local copies, waits for them, and re-layouts  29 us (6%)
  matrix products  17.3 us (4%)
    all_to_all x1, waiting for transfers between devices, per_device(): lax.all_to_all(jnp.stack([strips] * lax.axis_size('band')), 'band', 0, 0)  268 us
    ppermute x20, starting transfers between devices, passed_along(): return lax.ppermute(array, axis, pairs)  87 us
    dynamic_slice x32, local copies, waits for them, and re-layouts, per_device(): state, unused = lax.scan(advance, state, (blocks, starts))  25.9 us
    all_to_all x1, starting transfers between devices, per_device(): lax.all_to_all(jnp.stack([strips] * lax.axis_size('band')), 'band', 0, 0)  25.6 us
    ppermute x20, waiting for transfers between devices, passed_along(): return lax.ppermute(array, axis, pairs)  11.3 us
    dot_general x50, matrix products, conv_valid(): jnp.dot(tap_slice.reshape(-1, tap_slice.shape[-1]), weight[kernel_tap], p...  10.7 us
    div x16, other arithmetic, strip_step(): row_centre = strip_row.astype(jnp.float32) / total_rows  10.4 us
    add x16, other arithmetic, strip_step(): strip_row = row_zero + jnp.arange(block_rows, dtype=jnp.int32)  10.3 us
  transfers between devices with their start and end apart: 21, of which 6 were waited for; matrix products, arithmetic and copies ran while one was open for 1% of the time, Pallas kernels for 0%

profile of v1, /device:TPU:7, one launch (start us, length us, event | category | flops | bytes accessed | tf_op | source)
XLA Modules:
  0.0 479.6 jit_solution(16783379574916402410)
XLA Ops:
  0.6 1.0 convert_reduce_fusion
  1.7 3.1 stack.8
  4.8 25.6 %all-to-all-start = ((bf16[256,1,48,256]{3,2,1,0:T(8,128)(2,1)}), bf16[256,1,48,256]{3,2,1,0:T(8,128)(2,1)}, u32[]{:S(2)}, u32[]{:S(2)}) async-start(bf16[256,1,48,256]{3,2,1,0:T(8,128)(2,1)} %stack.8), calls=%async_computation | async-start | bytes 12582912 | tf_op jit(solution)/shard_map/all_to_all | solution.py:163
  31.3 268.3 %all-to-all-done = bf16[256,1,48,256]{3,2,1,0:T(8,128)(2,1)} async-done(((bf16[256,1,48,256]{3,2,1,0:T(8,128)(2,1)}), bf16[256,1,48,256]{3,2,1,0:T(8,128)(2,1)}, u32[]{:S(2)}, u32[]{:S(2)}) %all-to-all-start) | async-done | bytes 6291488 | tf_op jit(solution)/shard_map/all_to_all | solution.py:163
  299.7 70.1 %while.19 = (s32[]{:T(128)}, f32[384]{0:T(512)S(1)}, f32[384]{0:T(512)S(1)}, f32[384]{0:T(512)S(1)}, f32[384]{0:T(512)S(1)}, /*index=5*/f32[384]{0:T(512)S(1)}, ...) while((s32[]{:T(128)}, f32[384]{0:T(512)S(1)}, ...), condition=%wide.region_9.10_spmd.clone, body=%wide.region_1.9_spmd.clone.sunk | while | flops 153702400 | bytes 6978856 | solution.py:186
  299.7 1.1 constant_dynamic-slice_fusion.2
  303.2 0.7 convert_multiply_fusion.2
  304.1 1.0 constant_dynamic-slice_fusion.2
  308.5 1.0 constant_dynamic-slice_fusion.2
  312.8 1.0 constant_dynamic-slice_fusion.2
  317.2 1.0 constant_dynamic-slice_fusion.2
  321.6 1.0 constant_dynamic-slice_fusion.2
  326.0 1.0 constant_dynamic-slice_fusion.2
  330.4 1.0 constant_dynamic-slice_fusion.2
  334.7 1.0 constant_dynamic-slice_fusion.2
  339.1 1.0 constant_dynamic-slice_fusion.2
  343.5 1.0 constant_dynamic-slice_fusion.2
  347.9 1.0 constant_dynamic-slice_fusion.2
  352.2 1.0 constant_dynamic-slice_fusion.2
  356.6 1.0 constant_dynamic-slice_fusion.2
  361.0 1.0 constant_dynamic-slice_fusion.2
  365.4 1.0 constant_dynamic-slice_fusion.2
  372.6 9.8 %collective-permute-start.1 = (bf16[1,384,128]{2,1,0:T(8,128)(2,1)S(1)}, bf16[1,384,128]{2,1,0:T(8,128)(2,1)S(1)}, u32[]{:S(2)}, u32[]{:S(2)}) collective-permute-start(bf16[1,384,128]{2,1,0:T(8,128)(2,1)S(1)} %get-tuple-element.142), channel_id=1, source_target_pairs={{0,2},{2,4},{4,6},{6,8},{8,10},{10,12},{12,14},{14,16},{16,18},{18... | collective-permute-start | bytes 294920 | tf_op jit(solution)/shard_map/ppermute | solution.py:13
  382.4 1.9 collective-permute-start
  384.3 9.1 %collective-permute-start.3 = (bf16[1,384,128]{2,1,0:T(8,128)(2,1)S(1)}, bf16[1,384,128]{2,1,0:T(8,128)(2,1)S(1)}, u32[]{:S(2)}, u32[]{:S(2)}) collective-permute-start(bf16[1,384,128]{2,1,0:T(8,128)(2,1)S(1)} %get-tuple-element.142), channel_id=1, source_target_pairs={{4,0},{6,2},{8,4},{10,6},{12,8},{14,10},{16,12},{18,14},{20,16},{2... | collective-permute-start | bytes 294920 | tf_op jit(solution)/shard_map/ppermute | solution.py:13
  393.4 1.9 collective-permute-start.2
  395.4 3.6 collective-permute-start.5
  400.1 1.9 collective-permute-start.4
  402.2 9.1 %collective-permute-start.7 = (bf16[1,384,256]{2,1,0:T(8,128)(2,1)S(1)}, bf16[1,384,256]{2,1,0:T(8,128)(2,1)S(1)}, u32[]{:S(2)}, u32[]{:S(2)}) collective-permute-start(bf16[1,384,256]{2,1,0:T(8,128)(2,1)S(1)} %pad_maximum_fusion), channel_id=1, source_target_pairs={{4,0},{6,2},{8,4},{10,6},{12,8},{14,10},{16,12},{18,14},{20,16},{2... | collective-permute-start | bytes 589832 | tf_op jit(solution)/shard_map/ppermute | solution.py:13
  411.5 1.9 collective-permute-start.6
  414.2 1.8 collective-permute-done.7
  416.2 2.2 collective-permute-done.6
  419.1 1.9 collective-permute-start.9
  421.1 1.9 collective-permute-start.8
  423.1 9.1 %collective-permute-start.11 = (bf16[1,384,128]{2,1,0:T(8,128)(2,1)S(1)}, bf16[1,384,128]{2,1,0:T(8,128)(2,1)S(1)}, u32[]{:S(2)}, u32[]{:S(2)}) collective-permute-start(bf16[1,384,128]{2,1,0:T(8,128)(2,1)S(1)} %fusion.60), channel_id=1, source_target_pairs={{4,0},{6,2},{8,4},{10,6},{12,8},{14,10},{16,12},{18,14},{20,16},{2... | collective-permute-start | bytes 294920 | tf_op jit(solution)/shard_map/ppermute | solution.py:13
  432.2 3.0 collective-permute-start.10
  435.6 2.5 collective-permute-done.10
  440.3 1.9 collective-permute-start.13
  442.4 1.9 collective-permute-start.12
  444.3 9.1 %collective-permute-start.15 = (bf16[1,384,128]{2,1,0:T(8,128)(2,1)S(1)}, bf16[1,384,128]{2,1,0:T(8,128)(2,1)S(1)}, u32[]{:S(2)}, u32[]{:S(2)}) collective-permute-start(bf16[1,384,128]{2,1,0:T(8,128)(2,1)S(1)} %get-tuple-element.146), channel_id=1, source_target_pairs={{4,0},{6,2},{8,4},{10,6},{12,8},{14,10},{16,12},{18,14},{20,16},{2... | collective-permute-start | bytes 294920 | tf_op jit(solution)/shard_map/ppermute | solution.py:13
  453.4 3.0 collective-permute-start.14
  457.0 2.3 collective-permute-done.14
  459.6 1.9 collective-permute-start.17
  461.7 1.9 collective-permute-start.16
  463.7 9.1 %collective-permute-start.19 = (bf16[1,384,128]{2,1,0:T(8,128)(2,1)S(1)}, bf16[1,384,128]{2,1,0:T(8,128)(2,1)S(1)}, u32[]{:S(2)}, u32[]{:S(2)}) collective-permute-start(bf16[1,384,128]{2,1,0:T(8,128)(2,1)S(1)} %fusion.58), channel_id=1, source_target_pairs={{4,0},{6,2},{8,4},{10,6},{12,8},{14,10},{16,12},{18,14},{20,16},{2... | collective-permute-start | bytes 294920 | tf_op jit(solution)/shard_map/ppermute | solution.py:13
  472.8 3.0 collective-permute-start.18
  476.2 2.5 collective-permute-done.18
  478.7 0.9 multiply_add_fusion
  (369 shorter events, 62.7 us)
Async XLA Ops:
  4.8 25.7 %copy-start.6 = (f32[3,128]{1,0:T(4,128)S(1)}, f32[3,128]{1,0:T(4,128)}, u32[]{:S(2)}) copy-start(f32[3,128]{1,0:T(4,128)} %param.15) | copy-start | bytes 4612
  4.8 25.7 %copy-start.5 = (s32[2,1,384]{2,1,0:T(1,128)S(1)}, s32[2,1,384]{2,1,0:T(1,128)}, u32[]{:S(2)}) copy-start(s32[2,1,384]{2,1,0:T(1,128)} %param.14) | copy-start | bytes 9220
  4.8 25.7 %copy-start.1 = (bf16[1,384,128]{2,1,0:T(8,128)(2,1)S(1)}, bf16[1,384,128]{2,1,0:T(8,128)(2,1)}, u32[]{:S(2)}) copy-start(bf16[1,384,128]{2,1,0:T(8,128)(2,1)} %param.13) | copy-start | bytes 294916
  4.8 25.8 %copy-start.3 = (bf16[5,384,384]{2,1,0:T(8,128)(2,1)S(1)}, bf16[5,384,384]{2,1,0:T(8,128)(2,1)}, u32[]{:S(2)}) copy-start(bf16[5,384,384]{2,1,0:T(8,128)(2,1)} %param.16) | copy-start | bytes 4423684
  4.8 294.9 %all-to-all-start = ((bf16[256,1,48,256]{3,2,1,0:T(8,128)(2,1)}), bf16[256,1,48,256]{3,2,1,0:T(8,128)(2,1)}, u32[]{:S(2)}, u32[]{:S(2)}) async-start(bf16[256,1,48,256]{3,2,1,0:T(8,128)(2,1)} %stack.8), calls=%async_computation | async-start | bytes 12582912 | tf_op jit(solution)/shard_map/all_to_all | solution.py:163
  30.7 268.9 %copy-start = (bf16[1,384,256]{2,1,0:T(8,128)(2,1)S(1)}, bf16[1,384,256]{2,1,0:T(8,128)(2,1)}, u32[]{:S(2)}) copy-start(bf16[1,384,256]{2,1,0:T(8,128)(2,1)} %param.10) | copy-start | bytes 589828
  299.7 70.3 %copy-start.4 = (bf16[1,384,128]{2,1,0:T(8,128)(2,1)S(1)}, bf16[1,384,128]{2,1,0:T(8,128)(2,1)}, u32[]{:S(2)}) copy-start(bf16[1,384,128]{2,1,0:T(8,128)(2,1)} %param.12) | copy-start | bytes 294916
  371.7 27.3 %copy-start.2 = (bf16[5,384,384]{2,1,0:T(8,128)(2,1)S(1)}, bf16[5,384,384]{2,1,0:T(8,128)(2,1)}, u32[]{:S(2)}) copy-start(bf16[5,384,384]{2,1,0:T(8,128)(2,1)} %param.17) | copy-start | bytes 4423684
  372.6 27.5 %collective-permute-start.1 = (bf16[1,384,128]{2,1,0:T(8,128)(2,1)S(1)}, bf16[1,384,128]{2,1,0:T(8,128)(2,1)S(1)}, u32[]{:S(2)}, u32[]{:S(2)}) collective-permute-start(bf16[1,384,128]{2,1,0:T(8,128)(2,1)S(1)} %get-tuple-element.142), channel_id=1, source_target_pairs={{0,2},{2,4},{4,6},{6,8},{8,10},{10,12},{12,14},{14,16},{16,18},{18... | collective-permute-start | bytes 294920 | tf_op jit(solution)/shard_map/ppermute | solution.py:13
  382.4 19.8 %collective-permute-start = (bf16[1,384,128]{2,1,0:T(8,128)(2,1)S(1)}, bf16[1,384,128]{2,1,0:T(8,128)(2,1)S(1)}, u32[]{:S(2)}, u32[]{:S(2)}) collective-permute-start(bf16[1,384,128]{2,1,0:T(8,128)(2,1)S(1)} %get-tuple-element.142), channel_id=1, source_target_pairs={{0,4},{2,6},{4,8},{6,10},{8,12},{10,14},{12,16},{14,18},{16,20},{1... | collective-permute-start | bytes 294920 | tf_op jit(solution)/shard_map/ppermute | solution.py:13
  384.3 27.2 %collective-permute-start.3 = (bf16[1,384,128]{2,1,0:T(8,128)(2,1)S(1)}, bf16[1,384,128]{2,1,0:T(8,128)(2,1)S(1)}, u32[]{:S(2)}, u32[]{:S(2)}) collective-permute-start(bf16[1,384,128]{2,1,0:T(8,128)(2,1)S(1)} %get-tuple-element.142), channel_id=1, source_target_pairs={{4,0},{6,2},{8,4},{10,6},{12,8},{14,10},{16,12},{18,14},{20,16},{2... | collective-permute-start | bytes 294920 | tf_op jit(solution)/shard_map/ppermute | solution.py:13
  393.4 25.3 %collective-permute-start.2 = (bf16[1,384,128]{2,1,0:T(8,128)(2,1)S(1)}, bf16[1,384,128]{2,1,0:T(8,128)(2,1)S(1)}, u32[]{:S(2)}, u32[]{:S(2)}) collective-permute-start(bf16[1,384,128]{2,1,0:T(8,128)(2,1)S(1)} %get-tuple-element.142), channel_id=1, source_target_pairs={{2,0},{4,2},{6,4},{8,6},{10,8},{12,10},{14,12},{16,14},{18,16},{20... | collective-permute-start | bytes 294920 | tf_op jit(solution)/shard_map/ppermute | solution.py:13
  395.4 18.3 %collective-permute-start.5 = (bf16[1,384,256]{2,1,0:T(8,128)(2,1)S(1)}, bf16[1,384,256]{2,1,0:T(8,128)(2,1)S(1)}, u32[]{:S(2)}, u32[]{:S(2)}) collective-permute-start(bf16[1,384,256]{2,1,0:T(8,128)(2,1)S(1)} %pad_maximum_fusion), channel_id=1, source_target_pairs={{0,2},{2,4},{4,6},{6,8},{8,10},{10,12},{12,14},{14,16},{16,18},{18... | collective-permute-start | bytes 589832 | tf_op jit(solution)/shard_map/ppermute | solution.py:13
  400.1 13.8 %collective-permute-start.4 = (bf16[1,384,256]{2,1,0:T(8,128)(2,1)S(1)}, bf16[1,384,256]{2,1,0:T(8,128)(2,1)S(1)}, u32[]{:S(2)}, u32[]{:S(2)}) collective-permute-start(bf16[1,384,256]{2,1,0:T(8,128)(2,1)S(1)} %pad_maximum_fusion), channel_id=1, source_target_pairs={{0,4},{2,6},{4,8},{6,10},{8,12},{10,14},{12,16},{14,18},{16,20},{1... | collective-permute-start | bytes 589832 | tf_op jit(solution)/shard_map/ppermute | solution.py:13
  402.2 13.8 %collective-permute-start.7 = (bf16[1,384,256]{2,1,0:T(8,128)(2,1)S(1)}, bf16[1,384,256]{2,1,0:T(8,128)(2,1)S(1)}, u32[]{:S(2)}, u32[]{:S(2)}) collective-permute-start(bf16[1,384,256]{2,1,0:T(8,128)(2,1)S(1)} %pad_maximum_fusion), channel_id=1, source_target_pairs={{4,0},{6,2},{8,4},{10,6},{12,8},{14,10},{16,12},{18,14},{20,16},{2... | collective-permute-start | bytes 589832 | tf_op jit(solution)/shard_map/ppermute | solution.py:13
  411.5 7.0 %collective-permute-start.6 = (bf16[1,384,256]{2,1,0:T(8,128)(2,1)S(1)}, bf16[1,384,256]{2,1,0:T(8,128)(2,1)S(1)}, u32[]{:S(2)}, u32[]{:S(2)}) collective-permute-start(bf16[1,384,256]{2,1,0:T(8,128)(2,1)S(1)} %pad_maximum_fusion), channel_id=1, source_target_pairs={{2,0},{4,2},{6,4},{8,6},{10,8},{12,10},{14,12},{16,14},{18,16},{20... | collective-permute-start | bytes 589832 | tf_op jit(solution)/shard_map/ppermute | solution.py:13
  419.1 16.1 %collective-permute-start.9 = (bf16[1,384,128]{2,1,0:T(8,128)(2,1)S(1)}, bf16[1,384,128]{2,1,0:T(8,128)(2,1)S(1)}, u32[]{:S(2)}, u32[]{:S(2)}) collective-permute-start(bf16[1,384,128]{2,1,0:T(8,128)(2,1)S(1)} %fusion.60), channel_id=1, source_target_pairs={{0,2},{2,4},{4,6},{6,8},{8,10},{10,12},{12,14},{14,16},{16,18},{18... | collective-permute-start | bytes 294920 | tf_op jit(solution)/shard_map/ppermute | solution.py:13
  421.1 14.2 %collective-permute-start.8 = (bf16[1,384,128]{2,1,0:T(8,128)(2,1)S(1)}, bf16[1,384,128]{2,1,0:T(8,128)(2,1)S(1)}, u32[]{:S(2)}, u32[]{:S(2)}) collective-permute-start(bf16[1,384,128]{2,1,0:T(8,128)(2,1)S(1)} %fusion.60), channel_id=1, source_target_pairs={{0,4},{2,6},{4,8},{6,10},{8,12},{10,14},{12,16},{14,18},{16,20},{1... | collective-permute-start | bytes 294920 | tf_op jit(solution)/shard_map/ppermute | solution.py:13
  423.1 12.4 %collective-permute-start.11 = (bf16[1,384,128]{2,1,0:T(8,128)(2,1)S(1)}, bf16[1,384,128]{2,1,0:T(8,128)(2,1)S(1)}, u32[]{:S(2)}, u32[]{:S(2)}) collective-permute-start(bf16[1,384,128]{2,1,0:T(8,128)(2,1)S(1)} %fusion.60), channel_id=1, source_target_pairs={{4,0},{6,2},{8,4},{10,6},{12,8},{14,10},{16,12},{18,14},{20,16},{2... | collective-permute-start | bytes 294920 | tf_op jit(solution)/shard_map/ppermute | solution.py:13
  432.2 5.9 %collective-permute-start.10 = (bf16[1,384,128]{2,1,0:T(8,128)(2,1)S(1)}, bf16[1,384,128]{2,1,0:T(8,128)(2,1)S(1)}, u32[]{:S(2)}, u32[]{:S(2)}) collective-permute-start(bf16[1,384,128]{2,1,0:T(8,128)(2,1)S(1)} %fusion.60), channel_id=1, source_target_pairs={{2,0},{4,2},{6,4},{8,6},{10,8},{12,10},{14,12},{16,14},{18,16},{20... | collective-permute-start | bytes 294920 | tf_op jit(solution)/shard_map/ppermute | solution.py:13
  440.3 16.1 %collective-permute-start.13 = (bf16[1,384,128]{2,1,0:T(8,128)(2,1)S(1)}, bf16[1,384,128]{2,1,0:T(8,128)(2,1)S(1)}, u32[]{:S(2)}, u32[]{:S(2)}) collective-permute-start(bf16[1,384,128]{2,1,0:T(8,128)(2,1)S(1)} %get-tuple-element.146), channel_id=1, source_target_pairs={{0,2},{2,4},{4,6},{6,8},{8,10},{10,12},{12,14},{14,16},{16,18},{18... | collective-permute-start | bytes 294920 | tf_op jit(solution)/shard_map/ppermute | solution.py:13
  442.4 14.2 %collective-permute-start.12 = (bf16[1,384,128]{2,1,0:T(8,128)(2,1)S(1)}, bf16[1,384,128]{2,1,0:T(8,128)(2,1)S(1)}, u32[]{:S(2)}, u32[]{:S(2)}) collective-permute-start(bf16[1,384,128]{2,1,0:T(8,128)(2,1)S(1)} %get-tuple-element.146), channel_id=1, source_target_pairs={{0,4},{2,6},{4,8},{6,10},{8,12},{10,14},{12,16},{14,18},{16,20},{1... | collective-permute-start | bytes 294920 | tf_op jit(solution)/shard_map/ppermute | solution.py:13
  444.3 12.5 %collective-permute-start.15 = (bf16[1,384,128]{2,1,0:T(8,128)(2,1)S(1)}, bf16[1,384,128]{2,1,0:T(8,128)(2,1)S(1)}, u32[]{:S(2)}, u32[]{:S(2)}) collective-permute-start(bf16[1,384,128]{2,1,0:T(8,128)(2,1)S(1)} %get-tuple-element.146), channel_id=1, source_target_pairs={{4,0},{6,2},{8,4},{10,6},{12,8},{14,10},{16,12},{18,14},{20,16},{2... | collective-permute-start | bytes 294920 | tf_op jit(solution)/shard_map/ppermute | solution.py:13
  453.4 5.9 %collective-permute-start.14 = (bf16[1,384,128]{2,1,0:T(8,128)(2,1)S(1)}, bf16[1,384,128]{2,1,0:T(8,128)(2,1)S(1)}, u32[]{:S(2)}, u32[]{:S(2)}) collective-permute-start(bf16[1,384,128]{2,1,0:T(8,128)(2,1)S(1)} %get-tuple-element.146), channel_id=1, source_target_pairs={{2,0},{4,2},{6,4},{8,6},{10,8},{12,10},{14,12},{16,14},{18,16},{20... | collective-permute-start | bytes 294920 | tf_op jit(solution)/shard_map/ppermute | solution.py:13
  459.6 16.1 %collective-permute-start.17 = (bf16[1,384,128]{2,1,0:T(8,128)(2,1)S(1)}, bf16[1,384,128]{2,1,0:T(8,128)(2,1)S(1)}, u32[]{:S(2)}, u32[]{:S(2)}) collective-permute-start(bf16[1,384,128]{2,1,0:T(8,128)(2,1)S(1)} %fusion.58), channel_id=1, source_target_pairs={{0,2},{2,4},{4,6},{6,8},{8,10},{10,12},{12,14},{14,16},{16,18},{18... | collective-permute-start | bytes 294920 | tf_op jit(solution)/shard_map/ppermute | solution.py:13
  461.7 14.2 %collective-permute-start.16 = (bf16[1,384,128]{2,1,0:T(8,128)(2,1)S(1)}, bf16[1,384,128]{2,1,0:T(8,128)(2,1)S(1)}, u32[]{:S(2)}, u32[]{:S(2)}) collective-permute-start(bf16[1,384,128]{2,1,0:T(8,128)(2,1)S(1)} %fusion.58), channel_id=1, source_target_pairs={{0,4},{2,6},{4,8},{6,10},{8,12},{10,14},{12,16},{14,18},{16,20},{1... | collective-permute-start | bytes 294920 | tf_op jit(solution)/shard_map/ppermute | solution.py:13
  463.7 12.4 %collective-permute-start.19 = (bf16[1,384,128]{2,1,0:T(8,128)(2,1)S(1)}, bf16[1,384,128]{2,1,0:T(8,128)(2,1)S(1)}, u32[]{:S(2)}, u32[]{:S(2)}) collective-permute-start(bf16[1,384,128]{2,1,0:T(8,128)(2,1)S(1)} %fusion.58), channel_id=1, source_target_pairs={{4,0},{6,2},{8,4},{10,6},{12,8},{14,10},{16,12},{18,14},{20,16},{2... | collective-permute-start | bytes 294920 | tf_op jit(solution)/shard_map/ppermute | solution.py:13
  472.8 5.9 %collective-permute-start.18 = (bf16[1,384,128]{2,1,0:T(8,128)(2,1)S(1)}, bf16[1,384,128]{2,1,0:T(8,128)(2,1)S(1)}, u32[]{:S(2)}, u32[]{:S(2)}) collective-permute-start(bf16[1,384,128]{2,1,0:T(8,128)(2,1)S(1)} %fusion.58), channel_id=1, source_target_pairs={{2,0},{4,2},{6,4},{8,6},{10,8},{12,10},{14,12},{16,14},{18,16},{20... | collective-permute-start | bytes 294920 | tf_op jit(solution)/shard_map/ppermute | solution.py:13
